TPU v7x, 512 devices: a whole 4x4x16 slice. The times are simulated.
512 devices in a mesh: chan: 32 (over x_lo, z), freq: 16 (over y, x_hi, core).
Axes of the slice: x: 4 (x_hi: 2, x_lo: 2; x = x_hi * 2 + x_lo), y: 4, z: 16, core: 2. Of those that a mesh axis runs over, the one named last changes fastest.
Arguments:
- traces: bfloat16 [4096, 81920], P('chan', 'freq'), may hold values from -2000 to 2000
- kept_bins: int32 [128], replicated, may hold values from 1 to 255, as said below
- round_masks: int32 [2], replicated, may hold values from 1 to 31, as said below
Outputs:
- cross_spectra: float32 [2, 128, 2, 4096, 128], P(None, 'freq', None, 'chan')
- auto_spectra: float32 [128, 2, 4096, 128], P('freq', None, 'chan')
Inputs may be any that keep to these rules, and one draw needn't show every extreme that they name: `kept_bins`: 128 distinct bin numbers in increasing order; 1 and 255 are among them. `round_masks`: 2 distinct numbers; in round r channel block b is paired with block b XOR round_masks[r].
All inputs are finite; a program needn't handle non-finite values.
Results may differ from a plain program's by a relative error of at most 0.0066.
Values may be sent and summed in bfloat16 or wider, within the bound.
No kernel may reach another device: no remote copies, remote signals or barrier semaphores. Data moves between devices by JAX's collectives and lax.ppermute only.
A program may use at most 64 MiB of HBM per device.

v0:
```python
import math
import jax
import jax.numpy as jnp
from jax import lax
from jax.sharding import PartitionSpec as P

NS = 512
ROUNDS = 2
EPSILON = 1e-06


def shifted(block, axis, distance):
    devices = range(lax.axis_size(axis))
    route = [(i - distance, i) for i in devices if i - distance in devices]
    return lax.ppermute(block, axis, route)


def swapped(shard, axis, distance):
    return lax.ppermute(shard, axis, [(i, i ^ 1 << distance) for i in range(lax.axis_size(axis))])


def dft_table(kept_bins):
    sample_index = jnp.arange(NS, dtype=jnp.int32)
    phase_index = kept_bins[:, None] * sample_index[None, :] % NS
    angles = phase_index.astype(jnp.float32) * jnp.float32(2.0 * math.pi / NS)
    hann_taper = 0.5 - 0.5 * jnp.cos(
        sample_index.astype(jnp.float32) * jnp.float32(2.0 * math.pi / NS)
    )
    stacked = jnp.stack([hann_taper * jnp.cos(angles), -hann_taper * jnp.sin(angles)], axis=1)
    return stacked.reshape(kept_bins.shape[0] * 2, NS).astype(jnp.bfloat16)


def correlate(left_block, right_block, windows):
    products = jnp.einsum(
        "kpwc,kqwd->kpqcd", left_block, right_block, preferred_element_type=jnp.float32
    )
    real_part = products[:, 0, 0] + products[:, 1, 1]
    imag_part = products[:, 1, 0] - products[:, 0, 1]
    return jnp.stack([real_part, imag_part], axis=1) * (1.0 / math.sqrt(windows))


def body(traces, kept_bins, round_masks):
    channels, samples_here = traces.shape
    hop_length = NS // 2
    frames = samples_here // hop_length
    keep_count = kept_bins.shape[0]
    transform = dft_table(kept_bins)
    following = shifted(traces[:, :hop_length], "freq", -1)
    extended = jnp.concatenate([traces, following], axis=1).reshape(
        channels, frames + 1, hop_length
    )
    spectra = jnp.einsum(
        "kn,cjn->kjc",
        transform[:, :hop_length],
        extended[:, :-1],
        preferred_element_type=jnp.float32,
    )
    spectra = spectra + jnp.einsum(
        "kn,cjn->kjc",
        transform[:, hop_length:],
        extended[:, 1:],
        preferred_element_type=jnp.float32,
    )
    rounded = spectra.astype(jnp.bfloat16).reshape(keep_count, 2, frames * channels)
    windows = frames * lax.axis_size("freq")
    values = rounded.astype(jnp.float32).reshape(keep_count, 2, frames, channels)
    partial_power = jnp.sum(values * values, axis=(1, 2))
    power_mean = lax.psum(partial_power, "freq") / windows
    whitened = (values * lax.rsqrt(power_mean + EPSILON)[:, None, None, :]).astype(jnp.bfloat16)
    arrived_bins = lax.all_to_all(
        whitened.reshape(keep_count, 2, frames * channels),
        "freq",
        split_axis=0,
        concat_axis=2,
        tiled=True,
    )
    own_block = arrived_bins.reshape(-1, 2, windows, channels)
    auto_spectra = correlate(own_block, own_block, windows)
    blocks_count = lax.axis_size("chan")
    crosses = []
    levels = blocks_count.bit_length() - 1
    for round_no in range(ROUNDS):
        round_mask = round_masks[round_no]
        carried = own_block
        for which_bit in range(levels):
            arrived = swapped(carried, "chan", which_bit)
            chosen = jnp.bitwise_and(jnp.right_shift(round_mask, which_bit), 1) == 1
            carried = jnp.where(chosen, arrived, carried)
        crosses.append(correlate(own_block, carried, windows))
    return (jnp.stack(crosses), auto_spectra)


def solution(mesh):
    placed = (P("chan", "freq"), P(), P())
    return jax.shard_map(
        body,
        mesh=mesh,
        in_specs=placed,
        out_specs=(P(None, "freq", None, "chan", None), P("freq", None, "chan", None)),
        check_vma=False,
    )
```

profile of v0, /device:TPU:8, one launch (start us, length us, event | category | flops | bytes accessed | tf_op | source)
XLA Modules:
  0.0 897.9 jit_solution(6204677982949660020)
XLA Ops:
  7.2 1.8 copy.73
  9.0 4.3 collective-permute-start
  13.3 1.3 multiply_convert_fusion.2
  14.6 0.3 copy.75
  15.0 0.1 collective-permute-done
  15.2 0.6 fusion.23
  15.8 0.7 fusion
  16.6 0.8 reduce_sum.21
  17.4 1.8 convert_bitcast_fusion
  19.2 2.4 copy.77
  21.6 2.5 reshape.423
  24.1 141.0 %all-reduce.2.cloned.1.call-done = f32[128,128]{1,0:T(8,128)} async-done(((f32[128,128]{1,0:T(8,128)}), f32[128,128]{1,0:T(8,128)}) %all-reduce.2.cloned.1.call-update) | async-done | bytes 65552 | tf_op jit(solution)/shard_map/psum | solution.py:68
  165.1 0.9 add_rsqrt_fusion
  166.1 1.2 mul.152
  167.3 2.9 copy.80
  170.2 2.7 multiply_convert_fusion
  172.9 24.6 %all_to_all.15 = bf16[128,2,2560]{2,1,0:T(2,128)(2,1)S(1)} all-to-all(bf16[128,2,2560]{2,1,0:T(2,128)(2,1)S(1)} %multiply_convert_fusion), channel_id=1, replica_groups=mesh['chan'=32,'freq'=16] {'freq'}, dimensions={0} | all-to-all | bytes 2621440 | tf_op jit(solution)/shard_map/all_to_all | solution.py:70
  197.5 0.7 copy.106
  198.3 1.6 reshape.422
  199.9 3.3 collective-permute-start.1
  203.2 0.6 fusion.25
  205.1 28.3 %collective-permute-done.1 = bf16[8,2,320,128]{3,2,1,0:T(8,128)(2,1)S(1)} collective-permute-done((bf16[8,2,320,128]{3,2,1,0:T(8,128)(2,1)S(1)}, bf16[8,2,320,128]{3,2,1,0:T(8,128)(2,1)S(1)}, u32[]{:S(2)}, u32[]{:S(2)}) %collective-permute-start.1) | collective-permute-done | bytes 1310752 | tf_op jit(solution)/shard_map/ppermute | solution.py:19
  233.4 0.2 broadcast_select_fusion.4
  233.5 4.2 collective-permute-start.2
  237.7 2.6 collective-permute-start.6
  240.9 83.0 %collective-permute-done.2 = bf16[8,2,320,128]{3,2,1,0:T(8,128)(2,1)S(1)} collective-permute-done((bf16[8,2,320,128]{3,2,1,0:T(8,128)(2,1)S(1)}, bf16[8,2,320,128]{3,2,1,0:T(8,128)(2,1)S(1)}, u32[]{:S(2)}, u32[]{:S(2)}) %collective-permute-start.2) | collective-permute-done | bytes 1310752 | tf_op jit(solution)/shard_map/ppermute | solution.py:19
  324.0 0.1 broadcast_select_fusion.5
  324.1 7.6 collective-permute-start.3
  332.3 22.4 %collective-permute-done.6 = bf16[8,2,320,128]{3,2,1,0:T(8,128)(2,1)S(1)} collective-permute-done((bf16[8,2,320,128]{3,2,1,0:T(8,128)(2,1)S(1)}, bf16[8,2,320,128]{3,2,1,0:T(8,128)(2,1)S(1)}, u32[]{:S(2)}, u32[]{:S(2)}) %collective-permute-start.6) | collective-permute-done | bytes 1310752 | tf_op jit(solution)/shard_map/ppermute | solution.py:19
  354.9 33.1 %collective-permute-start.7 = (bf16[8,2,320,128]{3,2,1,0:T(8,128)(2,1)S(1)}, bf16[8,2,320,128]{3,2,1,0:T(8,128)(2,1)S(1)}, u32[]{:S(2)}, u32[]{:S(2)}) collective-permute-start(bf16[8,2,320,128]{3,2,1,0:T(8,128)(2,1)S(1)} %broadcast_select_fusion.1), channel_id=1, source_target_pairs={{0,64},{16,80},{32,96},{48,112},{64,0},{80,16},{96,32},{112,48},{1... | collective-permute-start | bytes 3932168 | tf_op jit(solution)/shard_map/ppermute | solution.py:19
  388.6 226.2 %collective-permute-done.3 = bf16[8,2,320,128]{3,2,1,0:T(8,128)(2,1)S(1)} collective-permute-done((bf16[8,2,320,128]{3,2,1,0:T(8,128)(2,1)S(1)}, bf16[8,2,320,128]{3,2,1,0:T(8,128)(2,1)S(1)}, u32[]{:S(2)}, u32[]{:S(2)}) %collective-permute-start.3) | collective-permute-done | bytes 1310752 | tf_op jit(solution)/shard_map/ppermute | solution.py:19
  614.9 10.5 %collective-permute-start.4 = (bf16[8,2,320,128]{3,2,1,0:T(8,128)(2,1)S(1)}, bf16[8,2,320,128]{3,2,1,0:T(8,128)(2,1)S(1)}, u32[]{:S(2)}, u32[]{:S(2)}) collective-permute-start(bf16[8,2,320,128]{3,2,1,0:T(8,128)(2,1)S(1)} %broadcast_select_fusion.6), channel_id=1, source_target_pairs={{0,128},{16,144},{32,160},{48,176},{64,192},{80,208},{96,224},{112... | collective-permute-start | bytes 3932168 | tf_op jit(solution)/shard_map/ppermute | solution.py:19
  626.1 43.4 %collective-permute-done.7 = bf16[8,2,320,128]{3,2,1,0:T(8,128)(2,1)S(1)} collective-permute-done((bf16[8,2,320,128]{3,2,1,0:T(8,128)(2,1)S(1)}, bf16[8,2,320,128]{3,2,1,0:T(8,128)(2,1)S(1)}, u32[]{:S(2)}, u32[]{:S(2)}) %collective-permute-start.7) | collective-permute-done | bytes 1310752 | tf_op jit(solution)/shard_map/ppermute | solution.py:19
  669.5 1.2 broadcast_select_fusion.2
  670.7 123.7 %collective-permute-start.8 = (bf16[8,2,320,128]{3,2,1,0:T(8,128)(2,1)}, bf16[8,2,320,128]{3,2,1,0:T(8,128)(2,1)}, u32[]{:S(2)}, u32[]{:S(2)}) collective-permute-start(bf16[8,2,320,128]{3,2,1,0:T(8,128)(2,1)} %broadcast_select_fusion.2), channel_id=1, source_target_pairs={{0,128},{16,144},{32,160},{48,176},{64,192},{80,208},{96,224},{112... | collective-permute-start | bytes 3932168 | tf_op jit(solution)/shard_map/ppermute | solution.py:19
  795.1 1.2 broadcast_select_fusion.7
  796.3 2.9 collective-permute-start.5
  801.1 1.6 reshape.427
  802.7 0.8 convolution_bitcast_fusion
  803.5 48.4 %collective-permute-done.8 = bf16[8,2,320,128]{3,2,1,0:T(8,128)(2,1)} collective-permute-done((bf16[8,2,320,128]{3,2,1,0:T(8,128)(2,1)}, bf16[8,2,320,128]{3,2,1,0:T(8,128)(2,1)}, u32[]{:S(2)}, u32[]{:S(2)}) %collective-permute-start.8) | collective-permute-done | bytes 1310752 | tf_op jit(solution)/shard_map/ppermute | solution.py:19
  851.9 2.5 broadcast_select_fusion.3
  854.4 2.7 collective-permute-start.9
  857.3 1.3 copy.88
  858.7 2.1 convolution_bitcast_fusion.2
  860.9 25.6 %collective-permute-done.9 = bf16[8,2,320,128]{3,2,1,0:T(8,128)(2,1)} collective-permute-done((bf16[8,2,320,128]{3,2,1,0:T(8,128)(2,1)}, bf16[8,2,320,128]{3,2,1,0:T(8,128)(2,1)}, u32[]{:S(2)}, u32[]{:S(2)}) %collective-permute-start.9) | collective-permute-done | bytes 1310752 | tf_op jit(solution)/shard_map/ppermute | solution.py:19
  886.5 2.1 convolution_bitcast_fusion.1
  889.0 0.2 pad_maximum_fusion
  889.2 1.8 copy.87
  (27 shorter events, 1.5 us)
Async XLA Ops:
  7.2 6.2 copy-start.2
  7.2 158.0 %all-reduce.2.cloned.1.call-start = ((), (), s32[]{:S(2)}) async-start(), calls=%async_computation.1 | async-start | bytes 131072 | tf_op jit(solution)/shard_map/psum | solution.py:68
  9.0 6.1 collective-permute-start
  167.3 2.9 copy-start
  198.3 4.9 copy-start.1
  199.9 33.5 %collective-permute-start.1 = (bf16[8,2,320,128]{3,2,1,0:T(8,128)(2,1)S(1)}, bf16[8,2,320,128]{3,2,1,0:T(8,128)(2,1)S(1)}, u32[]{:S(2)}, u32[]{:S(2)}) collective-permute-start(bf16[8,2,320,128]{3,2,1,0:T(8,128)(2,1)S(1)} %reshape.422), channel_id=1, source_target_pairs={{0,16},{16,0},{32,48},{48,32},{64,80},{80,64},{96,112},{112,96},{1... | collective-permute-start | bytes 3932168 | tf_op jit(solution)/shard_map/ppermute | solution.py:19
  233.5 90.4 %collective-permute-start.2 = (bf16[8,2,320,128]{3,2,1,0:T(8,128)(2,1)S(1)}, bf16[8,2,320,128]{3,2,1,0:T(8,128)(2,1)S(1)}, u32[]{:S(2)}, u32[]{:S(2)}) collective-permute-start(bf16[8,2,320,128]{3,2,1,0:T(8,128)(2,1)S(1)} %get-tuple-element.14), channel_id=1, source_target_pairs={{0,32},{16,48},{32,0},{48,16},{64,96},{80,112},{96,64},{112,80},{1... | collective-permute-start | bytes 3932168 | tf_op jit(solution)/shard_map/ppermute | solution.py:19
  237.7 117.0 %collective-permute-start.6 = (bf16[8,2,320,128]{3,2,1,0:T(8,128)(2,1)S(1)}, bf16[8,2,320,128]{3,2,1,0:T(8,128)(2,1)S(1)}, u32[]{:S(2)}, u32[]{:S(2)}) collective-permute-start(bf16[8,2,320,128]{3,2,1,0:T(8,128)(2,1)S(1)} %get-tuple-element.15), channel_id=1, source_target_pairs={{0,32},{16,48},{32,0},{48,16},{64,96},{80,112},{96,64},{112,80},{1... | collective-permute-start | bytes 3932168 | tf_op jit(solution)/shard_map/ppermute | solution.py:19
  324.1 290.7 %collective-permute-start.3 = (bf16[8,2,320,128]{3,2,1,0:T(8,128)(2,1)S(1)}, bf16[8,2,320,128]{3,2,1,0:T(8,128)(2,1)S(1)}, u32[]{:S(2)}, u32[]{:S(2)}) collective-permute-start(bf16[8,2,320,128]{3,2,1,0:T(8,128)(2,1)S(1)} %broadcast_select_fusion.5), channel_id=1, source_target_pairs={{0,64},{16,80},{32,96},{48,112},{64,0},{80,16},{96,32},{112,48},{1... | collective-permute-start | bytes 3932168 | tf_op jit(solution)/shard_map/ppermute | solution.py:19
  354.9 314.6 %collective-permute-start.7 = (bf16[8,2,320,128]{3,2,1,0:T(8,128)(2,1)S(1)}, bf16[8,2,320,128]{3,2,1,0:T(8,128)(2,1)S(1)}, u32[]{:S(2)}, u32[]{:S(2)}) collective-permute-start(bf16[8,2,320,128]{3,2,1,0:T(8,128)(2,1)S(1)} %broadcast_select_fusion.1), channel_id=1, source_target_pairs={{0,64},{16,80},{32,96},{48,112},{64,0},{80,16},{96,32},{112,48},{1... | collective-permute-start | bytes 3932168 | tf_op jit(solution)/shard_map/ppermute | solution.py:19
  614.9 180.1 %collective-permute-start.4 = (bf16[8,2,320,128]{3,2,1,0:T(8,128)(2,1)S(1)}, bf16[8,2,320,128]{3,2,1,0:T(8,128)(2,1)S(1)}, u32[]{:S(2)}, u32[]{:S(2)}) collective-permute-start(bf16[8,2,320,128]{3,2,1,0:T(8,128)(2,1)S(1)} %broadcast_select_fusion.6), channel_id=1, source_target_pairs={{0,128},{16,144},{32,160},{48,176},{64,192},{80,208},{96,224},{112... | collective-permute-start | bytes 3932168 | tf_op jit(solution)/shard_map/ppermute | solution.py:19
  670.7 181.2 %collective-permute-start.8 = (bf16[8,2,320,128]{3,2,1,0:T(8,128)(2,1)}, bf16[8,2,320,128]{3,2,1,0:T(8,128)(2,1)}, u32[]{:S(2)}, u32[]{:S(2)}) collective-permute-start(bf16[8,2,320,128]{3,2,1,0:T(8,128)(2,1)} %broadcast_select_fusion.2), channel_id=1, source_target_pairs={{0,128},{16,144},{32,160},{48,176},{64,192},{80,208},{96,224},{112... | collective-permute-start | bytes 3932168 | tf_op jit(solution)/shard_map/ppermute | solution.py:19
  796.3 62.4 %collective-permute-start.5 = (bf16[8,2,320,128]{3,2,1,0:T(8,128)(2,1)}, bf16[8,2,320,128]{3,2,1,0:T(8,128)(2,1)}, u32[]{:S(2)}, u32[]{:S(2)}) collective-permute-start(bf16[8,2,320,128]{3,2,1,0:T(8,128)(2,1)} %broadcast_select_fusion.7), channel_id=1, source_target_pairs={{0,256},{16,272},{32,288},{48,304},{64,320},{80,336},{96,352},{112... | collective-permute-start | bytes 3932168 | tf_op jit(solution)/shard_map/ppermute | solution.py:19
  854.4 32.1 %collective-permute-start.9 = (bf16[8,2,320,128]{3,2,1,0:T(8,128)(2,1)}, bf16[8,2,320,128]{3,2,1,0:T(8,128)(2,1)}, u32[]{:S(2)}, u32[]{:S(2)}) collective-permute-start(bf16[8,2,320,128]{3,2,1,0:T(8,128)(2,1)} %broadcast_select_fusion.3), channel_id=1, source_target_pairs={{0,256},{16,272},{32,288},{48,304},{64,320},{80,336},{96,352},{112... | collective-permute-start | bytes 3932168 | tf_op jit(solution)/shard_map/ppermute | solution.py:19
Sparse Core Ops, SparseCore 0:
  17.5 147.5 all-reduce.1
where the time goes:
time: 899 us; the launch traced here: 898 us
  waiting for transfers between devices  618 us (69%)
  starting transfers between devices  195 us (22%)
  blocking collectives  24.6 us (3%)
  between operations  20.8 us (2%)
  local copies, waits for them, and re-layouts  19.1 us (2%)
  other arithmetic  13.9 us (2%)
    ppermute x9, waiting for transfers between devices, swapped(): lax.ppermute(shard, axis, [(i, i ^ 1 << distance) for i in range(lax.axis...  477 us
    ppermute x9, starting transfers between devices, swapped(): lax.ppermute(shard, axis, [(i, i ^ 1 << distance) for i in range(lax.axis...  190 us
    psum x1, waiting for transfers between devices, body(): power_mean = lax.psum(partial_power, 'freq') / windows  141 us
    all_to_all x1, blocking collectives, body(): lax.all_to_all(whitened.reshape(keep_count, 2, frames * channels), 'freq'...  24.6 us
  transfers between devices with their start and end apart: 11, of which 9 were waited for; matrix products, arithmetic and copies ran while one was open for 2% of the time, Pallas kernels for 0%

commit v1 on v0

--- a/solution.py
+++ b/solution.py
@@ -7,6 +7,7 @@
 NS = 512
 ROUNDS = 2
 EPSILON = 1e-06
+list_groups_up = lambda inp, chip_axis: jnp.sum(lax.all_gather(inp, axis_name=chip_axis), 0)
 
 
 def shifted(block, axis, distance):
@@ -65,7 +66,7 @@
     windows = frames * lax.axis_size("freq")
     values = rounded.astype(jnp.float32).reshape(keep_count, 2, frames, channels)
     partial_power = jnp.sum(values * values, axis=(1, 2))
-    power_mean = lax.psum(partial_power, "freq") / windows
+    power_mean = list_groups_up(partial_power, "freq") / windows
     whitened = (values * lax.rsqrt(power_mean + EPSILON)[:, None, None, :]).astype(jnp.bfloat16)
     arrived_bins = lax.all_to_all(
         whitened.reshape(keep_count, 2, frames * channels),

time: 899 us -> 815 us (0.907)
  the two profiles are of different devices: /device:TPU:8 before, /device:TPU:10 now
where the time goes in v1:
time: 815 us; the launch traced here: 814 us
  waiting for transfers between devices  536 us (66%)
  starting transfers between devices  194 us (24%)
  blocking collectives  23.4 us (3%)
  between operations  20.8 us (3%)
  local copies, waits for them, and re-layouts  19.1 us (2%)
  other arithmetic  14.4 us (2%)
    ppermute x9, waiting for transfers between devices, swapped(): lax.ppermute(shard, axis, [(i, i ^ 1 << distance) for i in range(lax.axis...  477 us
    ppermute x9, starting transfers between devices, swapped(): lax.ppermute(shard, axis, [(i, i ^ 1 << distance) for i in range(lax.axis...  191 us
    all_gather x1, waiting for transfers between devices, lax.all_gather(inp, axis_name=chip_axis)  58.8 us
    all_to_all x1, blocking collectives, body(): lax.all_to_all(whitened.reshape(keep_count, 2, frames * channels), 'freq'...  23.4 us
  transfers between devices with their start and end apart: 11, of which 9 were waited for; matrix products, arithmetic and copies ran while one was open for 3% of the time, Pallas kernels for 0%

profile of v1, /device:TPU:10, one launch (start us, length us, event | category | flops | bytes accessed | tf_op | source)
XLA Modules:
  0.0 814.3 jit_solution(2783745657284500279)
XLA Ops:
  7.2 1.8 copy.88
  9.0 3.4 collective-permute-start
  12.4 1.3 multiply_convert_fusion.2
  13.7 0.3 copy.90
  14.1 0.1 collective-permute-done
  14.3 0.5 fusion.23
  14.9 0.7 fusion
  15.7 0.8 reduce_sum.30
  16.5 1.8 convert_bitcast_fusion
  18.3 2.4 copy.92
  20.7 2.5 reshape.427
  23.2 58.8 %all-gather.3.cloned.1.call-done = f32[2048,128]{1,0:T(8,128)} async-done(((f32[128,128]{1,0:T(8,128)}), f32[2048,128]{1,0:T(8,128)}) %all-gather.3.cloned.1.call-update) | async-done | bytes 1048592 | tf_op jit(solution)/shard_map/all_gather | solution.py:10
  82.1 1.3 reduce_sum.31
  83.5 1.2 mul.152
  84.7 2.9 copy.95
  87.6 2.7 multiply_convert_fusion
  90.3 23.4 %all_to_all.15 = bf16[128,2,2560]{2,1,0:T(2,128)(2,1)S(1)} all-to-all(bf16[128,2,2560]{2,1,0:T(2,128)(2,1)S(1)} %multiply_convert_fusion), channel_id=1, replica_groups=mesh['chan'=32,'freq'=16] {'freq'}, dimensions={0} | all-to-all | bytes 2621440 | tf_op jit(solution)/shard_map/all_to_all | solution.py:71
  113.7 0.7 copy.121
  114.4 1.6 reshape.426
  116.1 3.5 collective-permute-start.1
  119.5 0.6 fusion.25
  121.4 28.0 %collective-permute-done.1 = bf16[8,2,320,128]{3,2,1,0:T(8,128)(2,1)S(1)} collective-permute-done((bf16[8,2,320,128]{3,2,1,0:T(8,128)(2,1)S(1)}, bf16[8,2,320,128]{3,2,1,0:T(8,128)(2,1)S(1)}, u32[]{:S(2)}, u32[]{:S(2)}) %collective-permute-start.1) | collective-permute-done | bytes 1310752 | tf_op jit(solution)/shard_map/ppermute | solution.py:20
  149.4 0.2 broadcast_select_fusion.4
  149.6 4.5 collective-permute-start.2
  154.1 2.3 collective-permute-start.6
  157.0 83.2 %collective-permute-done.2 = bf16[8,2,320,128]{3,2,1,0:T(8,128)(2,1)S(1)} collective-permute-done((bf16[8,2,320,128]{3,2,1,0:T(8,128)(2,1)S(1)}, bf16[8,2,320,128]{3,2,1,0:T(8,128)(2,1)S(1)}, u32[]{:S(2)}, u32[]{:S(2)}) %collective-permute-start.2) | collective-permute-done | bytes 1310752 | tf_op jit(solution)/shard_map/ppermute | solution.py:20
  240.2 0.1 broadcast_select_fusion.5
  240.4 7.6 collective-permute-start.3
  248.7 22.6 %collective-permute-done.6 = bf16[8,2,320,128]{3,2,1,0:T(8,128)(2,1)S(1)} collective-permute-done((bf16[8,2,320,128]{3,2,1,0:T(8,128)(2,1)S(1)}, bf16[8,2,320,128]{3,2,1,0:T(8,128)(2,1)S(1)}, u32[]{:S(2)}, u32[]{:S(2)}) %collective-permute-start.6) | collective-permute-done | bytes 1310752 | tf_op jit(solution)/shard_map/ppermute | solution.py:20
  271.4 32.9 %collective-permute-start.7 = (bf16[8,2,320,128]{3,2,1,0:T(8,128)(2,1)S(1)}, bf16[8,2,320,128]{3,2,1,0:T(8,128)(2,1)S(1)}, u32[]{:S(2)}, u32[]{:S(2)}) collective-permute-start(bf16[8,2,320,128]{3,2,1,0:T(8,128)(2,1)S(1)} %broadcast_select_fusion.1), channel_id=1, source_target_pairs={{0,64},{16,80},{32,96},{48,112},{64,0},{80,16},{96,32},{112,48},{1... | collective-permute-start | bytes 3932168 | tf_op jit(solution)/shard_map/ppermute | solution.py:20
  304.9 225.9 %collective-permute-done.3 = bf16[8,2,320,128]{3,2,1,0:T(8,128)(2,1)S(1)} collective-permute-done((bf16[8,2,320,128]{3,2,1,0:T(8,128)(2,1)S(1)}, bf16[8,2,320,128]{3,2,1,0:T(8,128)(2,1)S(1)}, u32[]{:S(2)}, u32[]{:S(2)}) %collective-permute-start.3) | collective-permute-done | bytes 1310752 | tf_op jit(solution)/shard_map/ppermute | solution.py:20
  531.0 10.8 %collective-permute-start.4 = (bf16[8,2,320,128]{3,2,1,0:T(8,128)(2,1)S(1)}, bf16[8,2,320,128]{3,2,1,0:T(8,128)(2,1)S(1)}, u32[]{:S(2)}, u32[]{:S(2)}) collective-permute-start(bf16[8,2,320,128]{3,2,1,0:T(8,128)(2,1)S(1)} %broadcast_select_fusion.6), channel_id=1, source_target_pairs={{0,128},{16,144},{32,160},{48,176},{64,192},{80,208},{96,224},{112... | collective-permute-start | bytes 3932168 | tf_op jit(solution)/shard_map/ppermute | solution.py:20
  542.4 42.9 %collective-permute-done.7 = bf16[8,2,320,128]{3,2,1,0:T(8,128)(2,1)S(1)} collective-permute-done((bf16[8,2,320,128]{3,2,1,0:T(8,128)(2,1)S(1)}, bf16[8,2,320,128]{3,2,1,0:T(8,128)(2,1)S(1)}, u32[]{:S(2)}, u32[]{:S(2)}) %collective-permute-start.7) | collective-permute-done | bytes 1310752 | tf_op jit(solution)/shard_map/ppermute | solution.py:20
  585.3 1.2 broadcast_select_fusion.2
  586.5 124.2 %collective-permute-start.8 = (bf16[8,2,320,128]{3,2,1,0:T(8,128)(2,1)}, bf16[8,2,320,128]{3,2,1,0:T(8,128)(2,1)}, u32[]{:S(2)}, u32[]{:S(2)}) collective-permute-start(bf16[8,2,320,128]{3,2,1,0:T(8,128)(2,1)} %broadcast_select_fusion.2), channel_id=1, source_target_pairs={{0,128},{16,144},{32,160},{48,176},{64,192},{80,208},{96,224},{112... | collective-permute-start | bytes 3932168 | tf_op jit(solution)/shard_map/ppermute | solution.py:20
  711.4 1.2 broadcast_select_fusion.7
  712.6 2.6 collective-permute-start.5
  717.1 1.6 reshape.432
  718.8 0.8 convolution_bitcast_fusion
  719.6 48.7 %collective-permute-done.8 = bf16[8,2,320,128]{3,2,1,0:T(8,128)(2,1)} collective-permute-done((bf16[8,2,320,128]{3,2,1,0:T(8,128)(2,1)}, bf16[8,2,320,128]{3,2,1,0:T(8,128)(2,1)}, u32[]{:S(2)}, u32[]{:S(2)}) %collective-permute-start.8) | collective-permute-done | bytes 1310752 | tf_op jit(solution)/shard_map/ppermute | solution.py:20
  768.2 2.5 broadcast_select_fusion.3
  770.7 2.4 collective-permute-start.9
  773.4 1.3 copy.103
  774.7 2.1 convolution_bitcast_fusion.2
  777.0 25.9 %collective-permute-done.9 = bf16[8,2,320,128]{3,2,1,0:T(8,128)(2,1)} collective-permute-done((bf16[8,2,320,128]{3,2,1,0:T(8,128)(2,1)}, bf16[8,2,320,128]{3,2,1,0:T(8,128)(2,1)}, u32[]{:S(2)}, u32[]{:S(2)}) %collective-permute-start.9) | collective-permute-done | bytes 1310752 | tf_op jit(solution)/shard_map/ppermute | solution.py:20
  802.9 2.1 convolution_bitcast_fusion.1
  805.4 0.2 pad_maximum_fusion
  805.6 1.8 copy.102
  (28 shorter events, 1.5 us)
Async XLA Ops:
  7.2 5.3 copy-start.2
  7.2 74.9 %all-gather.3.cloned.1.call-start = ((), (), s32[]{:S(2)}) async-start(), calls=%async_computation.1 | async-start | bytes 1114112 | tf_op jit(solution)/shard_map/all_gather | solution.py:10
  9.0 5.2 collective-permute-start
  84.7 2.9 copy-start
  114.4 5.1 copy-start.1
  116.1 33.4 %collective-permute-start.1 = (bf16[8,2,320,128]{3,2,1,0:T(8,128)(2,1)S(1)}, bf16[8,2,320,128]{3,2,1,0:T(8,128)(2,1)S(1)}, u32[]{:S(2)}, u32[]{:S(2)}) collective-permute-start(bf16[8,2,320,128]{3,2,1,0:T(8,128)(2,1)S(1)} %reshape.426), channel_id=1, source_target_pairs={{0,16},{16,0},{32,48},{48,32},{64,80},{80,64},{96,112},{112,96},{1... | collective-permute-start | bytes 3932168 | tf_op jit(solution)/shard_map/ppermute | solution.py:20
  149.6 90.6 %collective-permute-start.2 = (bf16[8,2,320,128]{3,2,1,0:T(8,128)(2,1)S(1)}, bf16[8,2,320,128]{3,2,1,0:T(8,128)(2,1)S(1)}, u32[]{:S(2)}, u32[]{:S(2)}) collective-permute-start(bf16[8,2,320,128]{3,2,1,0:T(8,128)(2,1)S(1)} %get-tuple-element.16), channel_id=1, source_target_pairs={{0,32},{16,48},{32,0},{48,16},{64,96},{80,112},{96,64},{112,80},{1... | collective-permute-start | bytes 3932168 | tf_op jit(solution)/shard_map/ppermute | solution.py:20
  154.1 117.2 %collective-permute-start.6 = (bf16[8,2,320,128]{3,2,1,0:T(8,128)(2,1)S(1)}, bf16[8,2,320,128]{3,2,1,0:T(8,128)(2,1)S(1)}, u32[]{:S(2)}, u32[]{:S(2)}) collective-permute-start(bf16[8,2,320,128]{3,2,1,0:T(8,128)(2,1)S(1)} %get-tuple-element.17), channel_id=1, source_target_pairs={{0,32},{16,48},{32,0},{48,16},{64,96},{80,112},{96,64},{112,80},{1... | collective-permute-start | bytes 3932168 | tf_op jit(solution)/shard_map/ppermute | solution.py:20
  240.4 290.5 %collective-permute-start.3 = (bf16[8,2,320,128]{3,2,1,0:T(8,128)(2,1)S(1)}, bf16[8,2,320,128]{3,2,1,0:T(8,128)(2,1)S(1)}, u32[]{:S(2)}, u32[]{:S(2)}) collective-permute-start(bf16[8,2,320,128]{3,2,1,0:T(8,128)(2,1)S(1)} %broadcast_select_fusion.5), channel_id=1, source_target_pairs={{0,64},{16,80},{32,96},{48,112},{64,0},{80,16},{96,32},{112,48},{1... | collective-permute-start | bytes 3932168 | tf_op jit(solution)/shard_map/ppermute | solution.py:20
  271.4 313.9 %collective-permute-start.7 = (bf16[8,2,320,128]{3,2,1,0:T(8,128)(2,1)S(1)}, bf16[8,2,320,128]{3,2,1,0:T(8,128)(2,1)S(1)}, u32[]{:S(2)}, u32[]{:S(2)}) collective-permute-start(bf16[8,2,320,128]{3,2,1,0:T(8,128)(2,1)S(1)} %broadcast_select_fusion.1), channel_id=1, source_target_pairs={{0,64},{16,80},{32,96},{48,112},{64,0},{80,16},{96,32},{112,48},{1... | collective-permute-start | bytes 3932168 | tf_op jit(solution)/shard_map/ppermute | solution.py:20
  531.0 180.4 %collective-permute-start.4 = (bf16[8,2,320,128]{3,2,1,0:T(8,128)(2,1)S(1)}, bf16[8,2,320,128]{3,2,1,0:T(8,128)(2,1)S(1)}, u32[]{:S(2)}, u32[]{:S(2)}) collective-permute-start(bf16[8,2,320,128]{3,2,1,0:T(8,128)(2,1)S(1)} %broadcast_select_fusion.6), channel_id=1, source_target_pairs={{0,128},{16,144},{32,160},{48,176},{64,192},{80,208},{96,224},{112... | collective-permute-start | bytes 3932168 | tf_op jit(solution)/shard_map/ppermute | solution.py:20
  586.5 181.7 %collective-permute-start.8 = (bf16[8,2,320,128]{3,2,1,0:T(8,128)(2,1)}, bf16[8,2,320,128]{3,2,1,0:T(8,128)(2,1)}, u32[]{:S(2)}, u32[]{:S(2)}) collective-permute-start(bf16[8,2,320,128]{3,2,1,0:T(8,128)(2,1)} %broadcast_select_fusion.2), channel_id=1, source_target_pairs={{0,128},{16,144},{32,160},{48,176},{64,192},{80,208},{96,224},{112... | collective-permute-start | bytes 3932168 | tf_op jit(solution)/shard_map/ppermute | solution.py:20
  712.6 62.1 %collective-permute-start.5 = (bf16[8,2,320,128]{3,2,1,0:T(8,128)(2,1)}, bf16[8,2,320,128]{3,2,1,0:T(8,128)(2,1)}, u32[]{:S(2)}, u32[]{:S(2)}) collective-permute-start(bf16[8,2,320,128]{3,2,1,0:T(8,128)(2,1)} %broadcast_select_fusion.7), channel_id=1, source_target_pairs={{0,256},{16,272},{32,288},{48,304},{64,320},{80,336},{96,352},{112... | collective-permute-start | bytes 3932168 | tf_op jit(solution)/shard_map/ppermute | solution.py:20
  770.7 32.1 %collective-permute-start.9 = (bf16[8,2,320,128]{3,2,1,0:T(8,128)(2,1)}, bf16[8,2,320,128]{3,2,1,0:T(8,128)(2,1)}, u32[]{:S(2)}, u32[]{:S(2)}) collective-permute-start(bf16[8,2,320,128]{3,2,1,0:T(8,128)(2,1)} %broadcast_select_fusion.3), channel_id=1, source_target_pairs={{0,256},{16,272},{32,288},{48,304},{64,320},{80,336},{96,352},{112... | collective-permute-start | bytes 3932168 | tf_op jit(solution)/shard_map/ppermute | solution.py:20
Sparse Core Ops, SparseCore 0:
  16.6 65.4 all-gather.2
